TPU v7x, 256 devices: a whole 4x4x8 slice. The times are simulated.
256 devices in a mesh: ctx: 128 (over y, x, z), head: 2 (over core).
Axes of the slice: x: 4, y: 4, z: 8, core: 2. Of those that a mesh axis runs over, the one named last changes fastest.
Arguments:
- queries: bfloat16 [16384, 4096], P('ctx', 'head'), may hold values from -9 to 9
- key_rows: bfloat16 [16384, 4096], P('ctx', 'head'), may hold values from -9 to 9
- value_rows: bfloat16 [16384, 4096], P('ctx', 'head'), may hold values from -6 to 6
- offsets: int32 [3, 32], P(None, 'head'), may hold values from 0 to 3, as said below
- sublayer_norm_gain: float32 [4096], P('head'), may hold values from 0.25 to 1.75
- cotangent: bfloat16 [16384, 4096], P('ctx', 'head'), may hold values from -6 to 6
Outputs:
- normed: bfloat16 [16384, 4096], P('ctx', 'head')
- query_grad: bfloat16 [16384, 4096], P('ctx', 'head')
- key_grad: bfloat16 [16384, 4096], P('ctx', 'head')
- value_grad: bfloat16 [16384, 4096], P('ctx', 'head')
Inputs may be any that keep to these rules, and one draw needn't show every extreme that they name: Row l holds offsets of 0 to 2**l - 1, and each of these values belongs to exactly 32 / 2**l heads.
All inputs are finite; a program needn't handle non-finite values.
Results may differ from a plain program's by a relative error of at most 0.007.
Values may be sent and summed in bfloat16 or wider, within the bound.
No kernel may reach another device: no remote copies, remote signals or barrier semaphores. Data moves between devices by JAX's collectives and lax.ppermute only.
A program may use at most 192 MiB of HBM per device.

v0:
```python
from functools import partial, reduce
import math
import jax
import jax.numpy as jnp
from jax import lax
from jax.sharding import PartitionSpec as P

SEG0 = 512
NEG_FILL = -1e30
EPSILON = 1e-05


def pick_rows(source, mask_table, stride):
    count = source.shape[0] // stride
    shaped = source.reshape((count, stride) + source.shape[1:])
    chosen = mask_table.reshape((1, stride, mask_table.shape[1]) + (1,) * (source.ndim - 2))
    return jnp.sum(jnp.where(chosen, shaped, jnp.zeros((), source.dtype)), axis=1)


def put_rows(picked, mask_table, stride, filler):
    chosen = mask_table.reshape((1, stride, mask_table.shape[1]) + (1,) * (picked.ndim - 2))
    spread = jnp.where(chosen, picked[:, None], jnp.asarray(filler, picked.dtype))
    return spread.reshape((picked.shape[0] * stride,) + picked.shape[1:])


def gather_group(members, group_axes):
    if not group_axes:
        return members
    return tuple((lax.all_gather(part, group_axes, axis=0, tiled=True) for part in members))


def grad_block(
    query_seg, key_seg, value_seg, dout_seg, lse_seg, delta_seg, score_scale, want_query, want_keys
):
    lse_t = jnp.transpose(lse_seg, (0, 2, 1))[..., None]
    delta_t = jnp.transpose(delta_seg, (0, 2, 1))[..., None]
    scores = (
        jnp.einsum("sqhd,skhd->shqk", query_seg, key_seg, preferred_element_type=jnp.float32)
        * score_scale
    )
    probs = jnp.exp(scores - lse_t)
    dprobs = jnp.einsum("sqhd,skhd->shqk", dout_seg, value_seg, preferred_element_type=jnp.float32)
    dscores = (probs * (dprobs - delta_t)).astype(jnp.bfloat16)
    query_part = None
    key_part = None
    value_part = None
    if want_query:
        query_part = (
            jnp.einsum("shqk,skhd->sqhd", dscores, key_seg, preferred_element_type=jnp.float32)
            * score_scale
        )
    if want_keys:
        probs_half = probs.astype(jnp.bfloat16)
        key_part = (
            jnp.einsum("shqk,sqhd->skhd", dscores, query_seg, preferred_element_type=jnp.float32)
            * score_scale
        )
        value_part = jnp.einsum(
            "shqk,sqhd->skhd", probs_half, dout_seg, preferred_element_type=jnp.float32
        )
    return (query_part, key_part, value_part)


def on_device(queries, key_rows, value_rows, offsets, sublayer_norm_gain, cotangent, level_axes):
    tok_rows = queries.shape[0]
    head_local = offsets.shape[1]
    head_size = queries.shape[1] // head_local
    level_count = offsets.shape[0]
    feature_total_count = lax.axis_size("head") * queries.shape[1]
    score_scale = 1.0 / math.sqrt(head_size)
    shape3 = (tok_rows, head_local, head_size)
    query_all = queries.reshape(shape3)
    key_all = key_rows.reshape(shape3)
    value_all = value_rows.reshape(shape3)

    def level_layout(level_num):
        stride = 2**level_num
        picked_rows = tok_rows // stride
        group_bits = level_axes[level_num]
        seg_count = max(1, picked_rows // SEG0)
        mask_table = jnp.arange(stride, dtype=jnp.int32)[:, None] == offsets[level_num][None, :]
        return (stride, picked_rows, group_bits, seg_count, mask_table)

    stored = []
    maxima = []
    totals = []
    partials = []
    for level_num in range(level_count):
        stride, picked_rows, group_bits, seg_count, mask_table = level_layout(level_num)
        query_sel = pick_rows(query_all, mask_table, stride)
        key_sel = pick_rows(key_all, mask_table, stride)
        value_sel = pick_rows(value_all, mask_table, stride)
        key_group, value_group = gather_group((key_sel, value_sel), group_bits)
        stored.append((key_group, value_group))
        query_seg = query_sel.reshape(seg_count, -1, head_local, head_size)
        key_seg = key_group.reshape(seg_count, SEG0, head_local, head_size)
        value_seg = value_group.reshape(seg_count, SEG0, head_local, head_size)
        scores = (
            jnp.einsum("sqhd,skhd->shqk", query_seg, key_seg, preferred_element_type=jnp.float32)
            * score_scale
        )
        row_max = jnp.max(scores, axis=-1)
        weights = jnp.exp(scores - row_max[..., None])
        row_total = jnp.sum(weights, axis=-1)
        level_out = jnp.einsum(
            "shqk,skhd->sqhd",
            weights.astype(jnp.bfloat16),
            value_seg,
            preferred_element_type=jnp.float32,
        )
        flat_max = jnp.transpose(row_max, (0, 2, 1)).reshape(picked_rows, head_local)
        flat_total = jnp.transpose(row_total, (0, 2, 1)).reshape(picked_rows, head_local)
        maxima.append(put_rows(flat_max, mask_table, stride, NEG_FILL))
        totals.append(put_rows(flat_total, mask_table, stride, 0.0))
        partials.append(
            put_rows(level_out.reshape(picked_rows, head_local, head_size), mask_table, stride, 0.0)
        )
    top_max = reduce(jnp.maximum, maxima)
    factors = [jnp.exp(each_max - top_max) for each_max in maxima]
    total = factors[0] * totals[0]
    summed = factors[0][..., None] * partials[0]
    for level_num in range(1, level_count):
        total = total + factors[level_num] * totals[level_num]
        summed = summed + factors[level_num][..., None] * partials[level_num]
    attended = (summed / total[..., None]).astype(jnp.bfloat16)
    log_total = top_max + jnp.log(total)
    attended_rows_flattened = attended.reshape(tok_rows, -1).astype(jnp.float32)
    first_sum, second_sum = lax.psum(
        (
            jnp.sum(attended_rows_flattened, axis=1),
            jnp.sum(attended_rows_flattened * attended_rows_flattened, axis=1),
        ),
        "head",
    )
    feature_mean = first_sum / feature_total_count
    variance = second_sum / feature_total_count - feature_mean * feature_mean
    inverse_deviation = 1.0 / jnp.sqrt(variance + EPSILON)
    normalized_input = (attended_rows_flattened - feature_mean[:, None]) * inverse_deviation[
        :, None
    ]
    normed = (normalized_input * sublayer_norm_gain[None, :]).astype(jnp.bfloat16)
    normalized_gradient = cotangent.astype(jnp.float32) * sublayer_norm_gain[None, :]
    gradient_sum_first, gradient_sum_second = lax.psum(
        (
            jnp.sum(normalized_gradient, axis=1),
            jnp.sum(normalized_gradient * normalized_input, axis=1),
        ),
        "head",
    )
    attended_gradient = (
        (
            normalized_gradient
            - gradient_sum_first[:, None] / feature_total_count
            - normalized_input * gradient_sum_second[:, None] / feature_total_count
        )
        * inverse_deviation[:, None]
    ).astype(jnp.bfloat16)
    dout_all = attended_gradient.reshape(shape3)
    delta = jnp.sum(dout_all.astype(jnp.float32) * attended.astype(jnp.float32), axis=-1)
    query_acc = jnp.zeros(shape3, jnp.float32)
    key_acc = jnp.zeros(shape3, jnp.float32)
    value_acc = jnp.zeros(shape3, jnp.float32)
    for level_num in range(level_count):
        stride, picked_rows, group_bits, seg_count, mask_table = level_layout(level_num)
        query_sel = pick_rows(query_all, mask_table, stride)
        key_sel = pick_rows(key_all, mask_table, stride)
        value_sel = pick_rows(value_all, mask_table, stride)
        dout_sel = pick_rows(dout_all, mask_table, stride)
        lse_sel = pick_rows(log_total, mask_table, stride)
        delta_sel = pick_rows(delta, mask_table, stride)
        key_group, value_group = stored[level_num]
        query_seg = query_sel.reshape(seg_count, -1, head_local, head_size)
        dout_seg = dout_sel.reshape(seg_count, -1, head_local, head_size)
        lse_seg = lse_sel.reshape(seg_count, -1, head_local)
        delta_seg = delta_sel.reshape(seg_count, -1, head_local)
        key_seg = key_group.reshape(seg_count, SEG0, head_local, head_size)
        value_seg = value_group.reshape(seg_count, SEG0, head_local, head_size)
        query_part, unused_key, unused_value = grad_block(
            query_seg, key_seg, value_seg, dout_seg, lse_seg, delta_seg, score_scale, True, False
        )
        query_group, dout_group, lse_group, delta_group = gather_group(
            (query_sel, dout_sel, lse_sel, delta_sel), group_bits
        )
        unused_query, key_part, value_part = grad_block(
            query_group.reshape(seg_count, SEG0, head_local, head_size),
            key_sel.reshape(seg_count, -1, head_local, head_size),
            value_sel.reshape(seg_count, -1, head_local, head_size),
            dout_group.reshape(seg_count, SEG0, head_local, head_size),
            lse_group.reshape(seg_count, SEG0, head_local),
            delta_group.reshape(seg_count, SEG0, head_local),
            score_scale,
            False,
            True,
        )
        key_own = key_part.reshape(picked_rows, head_local, head_size)
        value_own = value_part.reshape(picked_rows, head_local, head_size)
        query_acc = query_acc + put_rows(
            query_part.reshape(picked_rows, head_local, head_size), mask_table, stride, 0.0
        )
        key_acc = key_acc + put_rows(key_own, mask_table, stride, 0.0)
        value_acc = value_acc + put_rows(value_own, mask_table, stride, 0.0)
    flat_shape = (tok_rows, head_local * head_size)
    query_grad = query_acc.astype(jnp.bfloat16).reshape(flat_shape)
    key_grad = key_acc.astype(jnp.bfloat16).reshape(flat_shape)
    value_grad = value_acc.astype(jnp.bfloat16).reshape(flat_shape)
    return (normed, query_grad, key_grad, value_grad)


def split_mesh(mesh, tok_rows, level_count):
    ctx_count = mesh.shape["ctx"]
    sizes = sorted({max(1, SEG0 * 2**level_num // tok_rows) for level_num in range(level_count)})
    factors = []
    done = 1
    for size in sizes:
        if size > done:
            factors.append(size // done)
            done = size
    factors.append(ctx_count // done)
    names = tuple((f"c{index}" for index in range(len(factors))))
    shape = tuple(reversed(factors)) + (mesh.shape["head"],)
    sub_mesh = jax.sharding.Mesh(mesh.devices.reshape(shape), tuple(reversed(names)) + ("head",))
    level_axes = []
    for level_num in range(level_count):
        size = max(1, SEG0 * 2**level_num // tok_rows)
        count = 0
        span = 1
        while span < size:
            span *= factors[count]
            count += 1
        level_axes.append(tuple(reversed(names[:count])))
    return (sub_mesh, tuple(reversed(names)), level_axes)


def solution(mesh):

    def run(queries, key_rows, value_rows, offsets, sublayer_norm_gain, cotangent):
        tok_rows = queries.shape[0] // mesh.shape["ctx"]
        sub_mesh, ctx_axes, level_axes = split_mesh(mesh, tok_rows, offsets.shape[0])
        rows = P(ctx_axes, "head")
        in_specs = (rows, rows, rows, P(None, "head"), P("head"), rows)
        out_specs = (rows, rows, rows, rows)
        body = partial(on_device, level_axes=level_axes)
        return jax.shard_map(
            body, mesh=sub_mesh, in_specs=in_specs, out_specs=out_specs, check_vma=False
        )(queries, key_rows, value_rows, offsets, sublayer_norm_gain, cotangent)

    return run
```

profile of v0, /device:TPU:10, one launch (start us, length us, event | category | flops | bytes accessed | tf_op | source)
XLA Modules:
  0.0 700.7 jit_solution(9627745844129497146)
XLA Ops:
  24.4 40.6 %all-gather.17.cloned.1.call-done = bf16[512,16,128]{2,0,1:T(8,128)(2,1)} async-done(((bf16[128,16,128]{2,0,1:T(8,128)(2,1)}), bf16[512,16,128]{2,0,1:T(8,128)(2,1)}) %all-gather.17.cloned.1.call-update) | async-done | bytes 2097168 | tf_op jit(solution)/shard_map/all_gather | solution.py:29
  65.0 2.4 multiply_reduce_fusion
  67.4 1.9 copy-done
  71.3 36.1 %all-gather.19.cloned.1.call-done = bf16[512,16,128]{2,0,1:T(8,128)(2,1)} async-done(((bf16[64,16,128]{2,0,1:T(8,128)(2,1)}), bf16[512,16,128]{2,0,1:T(8,128)(2,1)}) %all-gather.19.cloned.1.call-update) | async-done | bytes 2097168 | tf_op jit(solution)/shard_map/all_gather | solution.py:29
  107.3 2.5 multiply_reduce_fusion.1
  112.6 36.0 %all-gather.25.cloned.1.call-done = bf16[512,16,128]{2,0,1:T(8,128)(2,1)} async-done(((bf16[64,16,128]{2,0,1:T(8,128)(2,1)}), bf16[512,16,128]{2,0,1:T(8,128)(2,1)}) %all-gather.25.cloned.1.call-update) | async-done | bytes 2097168 | tf_op jit(solution)/shard_map/all_gather | solution.py:29
  148.6 2.2 convolution_bitcast_fusion.1
  153.0 66.3 %all-gather.21.cloned.1.call-done = bf16[512,16,128]{2,0,1:T(8,128)(2,1)} async-done(((bf16[32,16,128]{2,0,1:T(8,128)(2,1)}), bf16[512,16,128]{2,0,1:T(8,128)(2,1)}) %all-gather.21.cloned.1.call-update) | async-done | bytes 2097168 | tf_op jit(solution)/shard_map/all_gather | solution.py:29
  219.2 2.6 fusion.116
  229.9 59.6 %all-gather.27.cloned.1.call-done = bf16[512,16,128]{2,0,1:T(8,128)(2,1)} async-done(((bf16[32,16,128]{2,0,1:T(8,128)(2,1)}), bf16[512,16,128]{2,0,1:T(8,128)(2,1)}) %all-gather.27.cloned.1.call-update) | async-done | bytes 2097168 | tf_op jit(solution)/shard_map/all_gather | solution.py:29
  289.5 2.1 convolution_bitcast_fusion.3
  293.2 2.5 copy.275
  297.2 42.7 %all-gather.23.cloned.1.call-done = bf16[512,16,128]{2,0,1:T(8,128)(2,1)} async-done(((bf16[128,16,128]{2,0,1:T(8,128)(2,1)}), bf16[512,16,128]{2,0,1:T(8,128)(2,1)}) %all-gather.23.cloned.1.call-update) | async-done | bytes 2097168 | tf_op jit(solution)/shard_map/all_gather | solution.py:29
  342.8 6.2 convert_reduce_fusion
  349.0 2.5 copy.263
  351.5 3.1 all-reduce.1
  355.3 3.8 fusion.66
  359.2 3.1 all-reduce
  363.0 2.7 multiply_convert_fusion.4
  365.6 2.1 copy.294
  367.7 2.0 broadcast_select_fusion
  369.7 2.1 copy.309
  385.0 6.9 all-gather.29.cloned.1.call-done
  391.9 4.4 fusion.117
  396.3 37.9 %all-gather.33.cloned.1.call-done = bf16[512,16,128]{2,0,1:T(8,128)(2,1)} async-done(((bf16[64,16,128]{2,0,1:T(8,128)(2,1)}), bf16[512,16,128]{2,0,1:T(8,128)(2,1)}) %all-gather.33.cloned.1.call-update) | async-done | bytes 2097168 | tf_op jit(solution)/shard_map/all_gather | solution.py:29
  434.2 3.8 fusion.111
  442.1 2.0 copy.354
  444.1 2.1 fusion.35
  449.2 2.1 fusion.86
  459.9 24.8 %all-gather.1 = f32[8,64,16]{1,2,0:T(8,128)S(1)} all-gather(f32[1,64,16]{1,2,0:T(8,128)} %copy.335), channel_id=1, replica_groups=mesh['c3'=8,'c2'=2,'c1'=2,'c0'=4,'head'=2] {'c1','c0'}, dimensions={0}, use_global_device_ids=true | all-gather | bytes 36864 | tf_op jit(solution)/shard_map/all_gather | solution.py:29
  486.9 24.7 %all-gather = f32[8,64,16]{1,2,0:T(8,128)S(1)} all-gather(f32[1,64,16]{1,2,0:T(8,128)} %copy.331), channel_id=1, replica_groups=mesh['c3'=8,'c2'=2,'c1'=2,'c0'=4,'head'=2] {'c1','c0'}, dimensions={0}, use_global_device_ids=true | all-gather | bytes 36864 | tf_op jit(solution)/shard_map/all_gather | solution.py:29
  515.2 2.4 select_reduce_fusion.9
  526.4 32.3 %all-gather.2 = f32[16,32,16]{1,2,0:T(8,128)S(1)} all-gather(f32[1,32,16]{1,2,0:T(8,128)S(1)} %copy.341), channel_id=1, replica_groups=mesh['c3'=8,'c2'=2,'c1'=2,'c0'=4,'head'=2] {'c2','c1','c0'}, dimensions={0}, use_global_device_ids=true | all-gather | bytes 34816 | tf_op jit(solution)/shard_map/all_gather | solution.py:29
  561.0 31.9 %all-gather.3 = f32[16,32,16]{1,2,0:T(8,128)S(1)} all-gather(f32[1,32,16]{1,2,0:T(8,128)S(1)} %copy.345), channel_id=1, replica_groups=mesh['c3'=8,'c2'=2,'c1'=2,'c0'=4,'head'=2] {'c2','c1','c0'}, dimensions={0}, use_global_device_ids=true | all-gather | bytes 34816 | tf_op jit(solution)/shard_map/all_gather | solution.py:29
  597.8 4.1 fusion.33
  603.7 3.5 fusion.27
  611.0 14.2 %all_gather.61 = f32[512,16]{0,1:T(8,128)} all-gather(f32[128,16]{0,1:T(8,128)} %get-tuple-element.38), channel_id=1, replica_groups=mesh['c3'=8,'c2'=2,'c1'=2,'c0'=4,'head'=2] {'c0'}, dimensions={0}, use_global_device_ids=true | all-gather | bytes 40960 | tf_op jit(solution)/shard_map/all_gather | solution.py:29
  626.0 13.9 %all_gather.63 = f32[512,16]{0,1:T(8,128)} all-gather(f32[128,16]{0,1:T(8,128)S(1)} %broadcast_select_fusion.8), channel_id=1, replica_groups=mesh['c3'=8,'c2'=2,'c1'=2,'c0'=4,'head'=2] {'c0'}, dimensions={0}, use_global_device_ids=true | all-gather | bytes 40960 | tf_op jit(solution)/shard_map/all_gather | solution.py:29
  641.4 2.5 fusion.19
  644.0 6.0 fusion.21
  649.9 5.9 fusion.3
  655.8 6.7 convolution_multiply_fusion.1
  662.5 2.1 convolution_bitcast_fusion
  665.8 4.2 fusion.25
  674.9 2.2 convolution_bitcast_fusion.2
  677.2 3.4 fusion.31
  685.4 4.2 fusion.50
  689.6 2.0 copy.357
  (252 shorter events, 110.1 us)
Async XLA Ops:
  7.2 2.5 copy-start.15
  7.2 57.9 %all-gather.17.cloned.1.call-start = ((), (), s32[]{:S(2)}) async-start(), calls=%async_computation | async-start | bytes 2621440 | tf_op jit(solution)/shard_map/all_gather | solution.py:29
  8.0 13.4 %copy-start.39 = (pred[16]{0:T(512)(128)(4,1)}, pred[16]{0:T(512)(128)(4,1)S(1)}, u32[]{:S(2)}) copy-start(pred[16]{0:T(512)(128)(4,1)S(1)} %compare_bitcast_fusion) | copy-start | bytes 52
  8.0 2.2 copy-start.14
  12.1 95.3 %all-gather.19.cloned.1.call-start = ((), (), s32[]{:S(2)}) async-start(), calls=%async_computation.1 | async-start | bytes 2359296 | tf_op jit(solution)/shard_map/all_gather | solution.py:29
  13.2 9.5 %copy-start.46 = (pred[2,16]{1,0:T(4,128)(4,1)}, pred[2,16]{1,0:T(4,128)(4,1)S(1)}, u32[]{:S(2)}) copy-start(pred[2,16]{1,0:T(4,128)(4,1)S(1)} %iota_compare_fusion.1) | copy-start | bytes 100
  13.9 4.0 copy-start.10
  14.7 133.9 %all-gather.25.cloned.1.call-start = ((), (), s32[]{:S(2)}) async-start(), calls=%async_computation.4 | async-start | bytes 2359296 | tf_op jit(solution)/shard_map/all_gather | solution.py:29
  15.6 203.6 %all-gather.21.cloned.1.call-start = ((), (), s32[]{:S(2)}) async-start(), calls=%async_computation.2 | async-start | bytes 2228224 | tf_op jit(solution)/shard_map/all_gather | solution.py:29
  15.7 6.3 copy-start.47
  15.7 7.7 %copy-start.21 = (bf16[128,2048]{1,0:T(8,128)(2,1)S(1)}, bf16[128,2048]{1,0:T(8,128)(2,1)}, u32[]{:S(2)}) copy-start(bf16[128,2048]{1,0:T(8,128)(2,1)} %param.11) | copy-start | bytes 1572868
  16.3 8.1 %copy-start.17 = (bf16[32,16,128]{2,1,0:T(8,128)(2,1)}, bf16[32,16,128]{2,1,0:T(8,128)(2,1)S(1)}, u32[]{:S(2)}) copy-start(bf16[32,16,128]{2,1,0:T(8,128)(2,1)S(1)} %get-tuple-element.32) | copy-start | bytes 393220
  16.3 8.1 %copy-start.18 = (bf16[32,16,128]{2,1,0:T(8,128)(2,1)}, bf16[32,16,128]{2,1,0:T(8,128)(2,1)S(1)}, u32[]{:S(2)}) copy-start(bf16[32,16,128]{2,1,0:T(8,128)(2,1)S(1)} %get-tuple-element.31) | copy-start | bytes 393220
  16.3 48.7 %copy-start.6 = (bf16[128,16,128]{2,0,1:T(8,128)(2,1)S(1)}, bf16[128,16,128]{2,0,1:T(8,128)(2,1)}, u32[]{:S(2)}) copy-start(bf16[128,16,128]{2,0,1:T(8,128)(2,1)} %get-tuple-element.62) | copy-start | bytes 1572868
  17.1 272.4 %all-gather.27.cloned.1.call-start = ((), (), s32[]{:S(2)}) async-start(), calls=%async_computation.5 | async-start | bytes 2228224 | tf_op jit(solution)/shard_map/all_gather | solution.py:29
  17.9 322.1 %all-gather.23.cloned.1.call-start = ((), (), s32[]{:S(2)}) async-start(), calls=%async_computation.3 | async-start | bytes 2621440 | tf_op jit(solution)/shard_map/all_gather | solution.py:29
  18.4 373.5 %all-gather.29.cloned.1.call-start = ((), (), s32[]{:S(2)}) async-start(), calls=%async_computation.6 | async-start | bytes 2621440 | tf_op jit(solution)/shard_map/all_gather | solution.py:29
  19.2 415.0 %all-gather.33.cloned.1.call-start = ((), (), s32[]{:S(2)}) async-start(), calls=%async_computation.8 | async-start | bytes 2359296 | tf_op jit(solution)/shard_map/all_gather | solution.py:29
  20.0 621.3 %all-gather.37.cloned.1.call-start = ((), (), s32[]{:S(2)}) async-start(), calls=%async_computation.10 | async-start | bytes 2228224 | tf_op jit(solution)/shard_map/all_gather | solution.py:29
  20.8 629.1 %all-gather.31.cloned.1.call-start = ((), (), s32[]{:S(2)}) async-start(), calls=%async_computation.7 | async-start | bytes 2621440 | tf_op jit(solution)/shard_map/all_gather | solution.py:29
  22.0 45.4 %copy-start.27 = (pred[32,4,16]{2,1,0:T(4,128)(4,1)}, pred[32,4,16]{2,1,0:T(4,128)(4,1)S(1)}, u32[]{:S(2)}) copy-start(pred[32,4,16]{2,1,0:T(4,128)(4,1)S(1)} %broadcast_in_dim.468) | copy-start | bytes 6148
  67.4 2.0 copy-start
  67.4 3.8 copy-start.24
  109.9 38.8 %copy-start.23 = (f32[16,64]{1,0:T(8,128)}, f32[16,64]{1,0:T(8,128)S(1)}, u32[]{:S(2)}) copy-start(f32[16,64]{1,0:T(8,128)S(1)} %get-tuple-element.65) | copy-start | bytes 12292
  339.9 2.7 copy-start.12
  339.9 2.8 copy-start.25
  339.9 2.8 copy-start.33
  339.9 2.8 copy-start.34
  339.9 2.8 copy-start.35
  339.9 2.8 copy-start.36
  339.9 2.8 copy-start.40
  340.0 2.8 copy-start.41
  340.0 2.8 copy-start.43
  355.3 3.8 copy-start.48
  355.3 3.8 copy-start.49
  369.7 292.8 %all-gather.35.cloned.1.call-start = ((), (), s32[]{:S(2)}) async-start(), calls=%async_computation.9 | async-start | bytes 2359296 | tf_op jit(solution)/shard_map/all_gather | solution.py:29
  376.2 298.7 %all-gather.39.cloned.1.call-start = ((), (), s32[]{:S(2)}) async-start(), calls=%async_computation.11 | async-start | bytes 2228224 | tf_op jit(solution)/shard_map/all_gather | solution.py:29
  434.2 3.8 copy-start.22
  597.7 6.0 copy-start.31
  597.8 6.0 copy-start.32
  609.4 30.6 %copy-start.26 = (f32[16,128]{1,0:T(8,128)S(1)}, f32[16,128]{1,0:T(8,128)}, u32[]{:S(2)}) copy-start(f32[16,128]{1,0:T(8,128)} %copy-done.24) | copy-start | bytes 24580
  609.4 30.5 %copy-start.29 = (f32[16,128]{1,0:T(8,128)S(1)}, f32[16,128]{1,0:T(8,128)}, u32[]{:S(2)}) copy-start(f32[16,128]{1,0:T(8,128)} %fusion) | copy-start | bytes 24580
  611.0 32.9 %copy-start.2 = (bf16[512,16,128]{2,0,1:T(8,128)(2,1)S(1)}, bf16[512,16,128]{2,0,1:T(8,128)(2,1)}, u32[]{:S(2)}) copy-start(bf16[512,16,128]{2,0,1:T(8,128)(2,1)} %all-gather.17.cloned.1.call-done) | copy-start | bytes 6291460
  641.4 2.6 copy-start.37
  641.4 2.6 copy-start.38
  655.8 6.7 copy-start.1
  674.9 2.3 copy-start.3
  683.6 1.7 copy-start.7
  (15 other events, 18.5 us)
Sparse Core Ops, SparseCore 0:
  12.2 52.8 all-gather.16
  66.8 40.4 all-gather.18
  109.1 39.4 all-gather.24
  150.3 68.9 all-gather.20
  220.9 68.5 all-gather.26
  291.7 48.1 all-gather.22
  342.3 49.5 all-gather.28
  393.7 40.4 all-gather.32
  436.0 68.9 all-gather.36
  506.6 49.5 all-gather.30
  558.0 40.7 all-gather.34
  600.5 68.6 all-gather.38
where the time goes:
time: 707 us; the launch traced here: 701 us
  waiting for transfers between devices  327 us (46%)
  blocking collectives  148 us (21%)
  local copies, waits for them, and re-layouts  109 us (15%)
  matrix products  66.7 us (9%)
  other arithmetic  33.2 us (5%)
  between operations  15.3 us (2%)
    all_gather x12, waiting for transfers between devices, gather_group(): lax.all_gather(part, group_axes, axis=0, tiled=True)  326 us
    all_gather x6, blocking collectives, gather_group(): lax.all_gather(part, group_axes, axis=0, tiled=True)  142 us
    broadcast_in_dim x45, local copies, waits for them, and re-layouts, put_rows(): jnp.where(chosen, picked[:, None], jnp.asarray(filler, picked.dtype))  36.9 us
    unnamed x128, local copies, waits for them, and re-layouts  24.1 us
    dot_general x3, matrix products, grad_block(): jnp.einsum('shqk,sqhd->skhd', dscores, query_seg, preferred_element_type=...  14.3 us
  transfers between devices with their start and end apart: 12, of which 8 were waited for; matrix products, arithmetic and copies ran while one was open for 26% of the time, Pallas kernels for 0%

commit v1 on v0

--- a/solution.py
+++ b/solution.py
@@ -10,6 +10,13 @@
 EPSILON = 1e-05
 
 
+def all_by_exchange(x, mesh_axis, dim):
+    size = lax.axis_size(mesh_axis)
+    blocks = jnp.stack([x for _ in range(size)])
+    blocks = lax.all_to_all(blocks, mesh_axis, split_axis=0, concat_axis=0)
+    return jnp.concatenate(blocks, axis=dim)
+
+
 def pick_rows(source, mask_table, stride):
     count = source.shape[0] // stride
     shaped = source.reshape((count, stride) + source.shape[1:])
@@ -26,7 +33,7 @@
 def gather_group(members, group_axes):
     if not group_axes:
         return members
-    return tuple((lax.all_gather(part, group_axes, axis=0, tiled=True) for part in members))
+    return tuple((all_by_exchange(part, group_axes, 0) for part in members))
 
 
 def grad_block(

time: 707 us -> 839 us (1.19)
  waiting for transfers between devices: 327 us -> 417 us
  blocking collectives: 148 us -> 60.2 us
  starting transfers between devices: 1.13 us -> 84.3 us
  local copies, waits for them, and re-layouts: 109 us -> 169 us
  between operations: 15.3 us -> 2.11 us
  matrix products: 66.7 us -> 56.1 us
    all_to_all x0 -> x17, waiting for transfers between devices: none -> 417 us  [all_by_exchange(): blocks = lax.all_to_all(blocks, mesh_axis, split_axis=0, concat_axis=0)]
    all_gather x12 -> x0, waiting for transfers between devices: 326 us -> none  [gather_group(): lax.all_gather(part, group_axes, axis=0, tiled=True)]
    all_gather x6 -> x0, blocking collectives: 142 us -> none  [gather_group(): lax.all_gather(part, group_axes, axis=0, tiled=True)]
    all_to_all x0 -> x17, starting transfers between devices: none -> 84.3 us  [all_by_exchange(): blocks = lax.all_to_all(blocks, mesh_axis, split_axis=0, concat_axis=0)]
    all_to_all x0 -> x1, blocking collectives: none -> 54 us  [all_by_exchange(): blocks = lax.all_to_all(blocks, mesh_axis, split_axis=0, concat_axis=0)]
    another operation x4 -> x20, local copies, waits for them, and re-layouts: 2.92 us -> 32.6 us  [the longest x14 28.5 us: all_by_exchange(): blocks = jnp.stack([x for _ in range(size)])]
    all_to_all x0 -> x18, local copies, waits for them, and re-layouts: none -> 26.5 us  [all_by_exchange(): blocks = lax.all_to_all(blocks, mesh_axis, split_axis=0, concat_axis=0)]
    mul x0 -> x6, local copies, waits for them, and re-layouts: none -> 13 us  [the longest x4 8.63 us: on_device(): summed = summed + factors[level_num][..., None] * partials[level_num]]
  transfers between devices with their start and end apart: 12 -> 17, of which waited for: 8 -> 15; matrix products, arithmetic and copies ran while one was open for 26% -> 25% of each run, Pallas kernels for 0% -> 0%
where the time goes in v1:
time: 839 us; the launch traced here: 828 us
  waiting for transfers between devices  417 us (50%)
  local copies, waits for them, and re-layouts  169 us (20%)
  starting transfers between devices  84.3 us (10%)
  blocking collectives  60.2 us (7%)
  matrix products  56.1 us (7%)
  other arithmetic  38.6 us (5%)
    all_to_all x17, waiting for transfers between devices, all_by_exchange(): blocks = lax.all_to_all(blocks, mesh_axis, split_axis=0, concat_axis=0)  417 us
    all_to_all x17, starting transfers between devices, all_by_exchange(): blocks = lax.all_to_all(blocks, mesh_axis, split_axis=0, concat_axis=0)  84.3 us
    all_to_all x1, blocking collectives, all_by_exchange(): blocks = lax.all_to_all(blocks, mesh_axis, split_axis=0, concat_axis=0)  54 us
    broadcast_in_dim x39, local copies, waits for them, and re-layouts, put_rows(): jnp.where(chosen, picked[:, None], jnp.asarray(filler, picked.dtype))  29 us
    another operation x14, local copies, waits for them, and re-layouts, all_by_exchange(): blocks = jnp.stack([x for _ in range(size)])  28.5 us
    unnamed x155, local copies, waits for them, and re-layouts  28 us
    all_to_all x18, local copies, waits for them, and re-layouts, all_by_exchange(): blocks = lax.all_to_all(blocks, mesh_axis, split_axis=0, concat_axis=0)  26.5 us
  transfers between devices with their start and end apart: 17, of which 15 were waited for; matrix products, arithmetic and copies ran while one was open for 25% of the time, Pallas kernels for 0%

profile of v1, /device:TPU:10, one launch (start us, length us, event | category | flops | bytes accessed | tf_op | source)
XLA Modules:
  0.0 828.0 jit_solution(2458320936791799907)
XLA Ops:
  5.4 54.0 %all_to_all.90 = bf16[4,128,16,128]{3,1,2,0:T(8,128)(2,1)} all-to-all(bf16[4,128,16,128]{3,1,2,0:T(8,128)(2,1)S(1)} %stack.36), channel_id=1, replica_groups=mesh['c3'=8,'c2'=2,'c1'=2,'c0'=4,'head'=2] {'c0'}, dimensions={0} | all-to-all | bytes 4194304 | tf_op jit(solution)/shard_map/all_to_all | solution.py:16
  61.3 3.6 all-to-all-start.3
  65.2 47.1 %all-to-all-done.3 = bf16[4,128,16,128]{1,3,2,0:T(8,128)(2,1)S(1)} async-done(((bf16[4,128,16,128]{1,3,2,0:T(8,128)(2,1)}), bf16[4,128,16,128]{1,3,2,0:T(8,128)(2,1)S(1)}, u32[]{:S(2)}, u32[]{:S(2)}) %all-to-all-start.3) | async-done | bytes 2097184 | tf_op jit(solution)/shard_map/all_to_all | solution.py:16
  114.2 3.6 all-to-all-start.6
  123.2 42.3 %all-to-all-done.6 = bf16[4,128,16,128]{3,1,2,0:T(8,128)(2,1)S(1)} async-done(((bf16[4,128,16,128]{3,1,2,0:T(8,128)(2,1)}), bf16[4,128,16,128]{3,1,2,0:T(8,128)(2,1)S(1)}, u32[]{:S(2)}, u32[]{:S(2)}) %all-to-all-start.6) | async-done | bytes 2097184 | tf_op jit(solution)/shard_map/all_to_all | solution.py:16
  168.6 6.6 all-to-all-start.1
  175.2 50.6 %all-to-all-done.1 = bf16[8,64,16,128]{3,1,2,0:T(8,128)(2,1)} async-done(((bf16[8,64,16,128]{3,1,2,0:T(8,128)(2,1)}), bf16[8,64,16,128]{3,1,2,0:T(8,128)(2,1)}, u32[]{:S(2)}, u32[]{:S(2)}) %all-to-all-start.1) | async-done | bytes 2097184 | tf_op jit(solution)/shard_map/all_to_all | solution.py:16
  227.6 3.6 all-to-all-start.4
  233.0 49.8 %all-to-all-done.4 = bf16[8,64,16,128]{3,1,2,0:T(8,128)(2,1)S(1)} async-done(((bf16[8,64,16,128]{3,1,2,0:T(8,128)(2,1)}), bf16[8,64,16,128]{3,1,2,0:T(8,128)(2,1)S(1)}, u32[]{:S(2)}, u32[]{:S(2)}) %all-to-all-start.4) | async-done | bytes 2097184 | tf_op jit(solution)/shard_map/all_to_all | solution.py:16
  285.8 3.6 all-to-all-start.10
  292.5 46.4 %all-to-all-done.10 = bf16[8,64,16,128]{3,1,2,0:T(8,128)(2,1)S(1)} async-done(((bf16[8,64,16,128]{3,1,2,0:T(8,128)(2,1)}), bf16[8,64,16,128]{3,1,2,0:T(8,128)(2,1)S(1)}, u32[]{:S(2)}, u32[]{:S(2)}) %all-to-all-start.10) | async-done | bytes 2097184 | tf_op jit(solution)/shard_map/all_to_all | solution.py:16
  340.9 4.7 all-to-all-start.2
  345.7 47.6 %all-to-all-done.2 = bf16[16,32,16,128]{3,1,2,0:T(8,128)(2,1)} async-done(((bf16[16,32,16,128]{3,1,2,0:T(8,128)(2,1)}), bf16[16,32,16,128]{3,1,2,0:T(8,128)(2,1)}, u32[]{:S(2)}, u32[]{:S(2)}) %all-to-all-start.2) | async-done | bytes 2097184 | tf_op jit(solution)/shard_map/all_to_all | solution.py:16
  395.1 8.5 %all-to-all-start.5 = ((bf16[16,32,16,128]{3,1,2,0:T(8,128)(2,1)}), bf16[16,32,16,128]{3,1,2,0:T(8,128)(2,1)}, u32[]{:S(2)}, u32[]{:S(2)}) async-start(bf16[16,32,16,128]{3,1,2,0:T(8,128)(2,1)} %stack.41), calls=%async_computation.5 | async-start | bytes 4194304 | tf_op jit(solution)/shard_map/all_to_all | solution.py:16
  424.6 3.5 copy.325
  428.1 23.3 %all-to-all-done.5 = bf16[16,32,16,128]{3,1,2,0:T(8,128)(2,1)} async-done(((bf16[16,32,16,128]{3,1,2,0:T(8,128)(2,1)}), bf16[16,32,16,128]{3,1,2,0:T(8,128)(2,1)}, u32[]{:S(2)}, u32[]{:S(2)}) %all-to-all-start.5) | async-done | bytes 2097184 | tf_op jit(solution)/shard_map/all_to_all | solution.py:16
  454.1 7.5 all-to-all-start.14
  479.8 6.5 convert_reduce_fusion
  506.1 3.1 all-reduce.1
  509.9 6.0 fusion.69
  515.8 3.1 all-reduce
  548.8 4.5 all-to-all-start.7
  554.1 5.0 all-to-all-done.7
  559.7 3.9 all-to-all-start.9
  569.3 6.0 all-to-all-start.11
  578.9 4.5 all-to-all-done.11
  583.4 3.9 all-to-all-start.13
  590.4 4.9 all-to-all-done.13
  595.3 4.5 all-to-all-start.15
  602.1 5.0 all-to-all-done.15
  607.1 5.2 all-to-all-start.17
  614.2 5.4 all-to-all-done.17
  622.6 4.6 all-to-all-start.8
  630.9 38.0 %all-to-all-done.8 = bf16[4,128,16,128]{1,3,2,0:T(8,128)(2,1)} async-done(((bf16[4,128,16,128]{1,3,2,0:T(8,128)(2,1)}), bf16[4,128,16,128]{1,3,2,0:T(8,128)(2,1)}, u32[]{:S(2)}, u32[]{:S(2)}) %all-to-all-start.8) | async-done | bytes 2097184 | tf_op jit(solution)/shard_map/all_to_all | solution.py:16
  671.8 4.4 all-to-all-start.12
  676.2 3.3 copy.398
  681.0 44.6 %all-to-all-done.12 = bf16[8,64,16,128]{3,1,2,0:T(8,128)(2,1)} async-done(((bf16[8,64,16,128]{3,1,2,0:T(8,128)(2,1)}), bf16[8,64,16,128]{3,1,2,0:T(8,128)(2,1)}, u32[]{:S(2)}, u32[]{:S(2)}) %all-to-all-start.12) | async-done | bytes 2097184 | tf_op jit(solution)/shard_map/all_to_all | solution.py:16
  728.2 5.7 all-to-all-start.16
  733.9 4.5 fusion.119
  741.5 6.7 convolution_multiply_fusion.2
  750.7 4.3 fusion.31
  758.0 3.4 fusion.37
  778.4 4.0 copy.401
  782.3 6.3 convolution_multiply_fusion.1
  791.3 4.8 fusion.3
  798.7 3.3 copy.412
  802.0 4.2 fusion.29
  823.7 3.8 fusion.43
  (311 shorter events, 202.4 us)
Async XLA Ops:
  0.6 3.4 copy-start.35
  1.4 406.3 %copy-start.55 = (pred[16]{0:T(512)(128)(4,1)}, pred[16]{0:T(512)(128)(4,1)S(1)}, u32[]{:S(2)}) copy-start(pred[16]{0:T(512)(128)(4,1)S(1)} %compare_bitcast_fusion) | copy-start | bytes 52
  4.5 54.9 %copy-start.20 = (bf16[128,16,128]{0,2,1:T(8,128)(2,1)}, bf16[128,16,128]{0,2,1:T(8,128)(2,1)S(1)}, u32[]{:S(2)}) copy-start(bf16[128,16,128]{0,2,1:T(8,128)(2,1)S(1)} %get-tuple-element.44) | copy-start | bytes 1572868
  4.5 54.9 %copy-start.37 = (bf16[128,16,128]{0,2,1:T(8,128)(2,1)}, bf16[128,16,128]{0,2,1:T(8,128)(2,1)S(1)}, u32[]{:S(2)}) copy-start(bf16[128,16,128]{0,2,1:T(8,128)(2,1)S(1)} %get-tuple-element.43) | copy-start | bytes 1572868
  4.5 60.4 %copy-start.21 = (bf16[128,16,128]{0,2,1:T(8,128)(2,1)}, bf16[128,16,128]{0,2,1:T(8,128)(2,1)S(1)}, u32[]{:S(2)}) copy-start(bf16[128,16,128]{0,2,1:T(8,128)(2,1)S(1)} %get-tuple-element.45) | copy-start | bytes 1572868
  61.3 51.0 %all-to-all-start.3 = ((bf16[4,128,16,128]{1,3,2,0:T(8,128)(2,1)}), bf16[4,128,16,128]{1,3,2,0:T(8,128)(2,1)S(1)}, u32[]{:S(2)}, u32[]{:S(2)}) async-start(bf16[4,128,16,128]{1,3,2,0:T(8,128)(2,1)} %stack.39), calls=%async_computation.3 | async-start | bytes 4194304 | tf_op jit(solution)/shard_map/all_to_all | solution.py:16
  114.2 51.3 %all-to-all-start.6 = ((bf16[4,128,16,128]{3,1,2,0:T(8,128)(2,1)}), bf16[4,128,16,128]{3,1,2,0:T(8,128)(2,1)S(1)}, u32[]{:S(2)}, u32[]{:S(2)}) async-start(bf16[4,128,16,128]{3,1,2,0:T(8,128)(2,1)} %stack.42), calls=%async_computation.6 | async-start | bytes 4194304 | tf_op jit(solution)/shard_map/all_to_all | solution.py:16
  120.4 283.4 %copy-start.60 = (pred[2,16]{1,0:T(4,128)(4,1)}, pred[2,16]{1,0:T(4,128)(4,1)S(1)}, u32[]{:S(2)}) copy-start(pred[2,16]{1,0:T(4,128)(4,1)S(1)} %iota_compare_fusion.1) | copy-start | bytes 100
  165.6 3.0 copy-start.11
  168.6 57.2 %all-to-all-start.1 = ((bf16[8,64,16,128]{3,1,2,0:T(8,128)(2,1)}), bf16[8,64,16,128]{3,1,2,0:T(8,128)(2,1)}, u32[]{:S(2)}, u32[]{:S(2)}) async-start(bf16[8,64,16,128]{3,1,2,0:T(8,128)(2,1)} %stack.37), calls=%async_computation.1 | async-start | bytes 4194304 | tf_op jit(solution)/shard_map/all_to_all | solution.py:16
  227.6 55.1 %all-to-all-start.4 = ((bf16[8,64,16,128]{3,1,2,0:T(8,128)(2,1)}), bf16[8,64,16,128]{3,1,2,0:T(8,128)(2,1)S(1)}, u32[]{:S(2)}, u32[]{:S(2)}) async-start(bf16[8,64,16,128]{3,1,2,0:T(8,128)(2,1)} %stack.40), calls=%async_computation.4 | async-start | bytes 4194304 | tf_op jit(solution)/shard_map/all_to_all | solution.py:16
  282.8 3.0 copy-start.15
  285.8 53.1 %all-to-all-start.10 = ((bf16[8,64,16,128]{3,1,2,0:T(8,128)(2,1)}), bf16[8,64,16,128]{3,1,2,0:T(8,128)(2,1)S(1)}, u32[]{:S(2)}, u32[]{:S(2)}) async-start(bf16[8,64,16,128]{3,1,2,0:T(8,128)(2,1)} %stack.46), calls=%async_computation.10 | async-start | bytes 4194304 | tf_op jit(solution)/shard_map/all_to_all | solution.py:16
  289.4 114.2 %copy-start.62 = (pred[4,16]{1,0:T(4,128)(4,1)}, pred[4,16]{1,0:T(4,128)(4,1)S(1)}, u32[]{:S(2)}) copy-start(pred[4,16]{1,0:T(4,128)(4,1)S(1)} %iota_compare_fusion) | copy-start | bytes 196
  340.9 52.4 %all-to-all-start.2 = ((bf16[16,32,16,128]{3,1,2,0:T(8,128)(2,1)}), bf16[16,32,16,128]{3,1,2,0:T(8,128)(2,1)}, u32[]{:S(2)}, u32[]{:S(2)}) async-start(bf16[16,32,16,128]{3,1,2,0:T(8,128)(2,1)} %stack.38), calls=%async_computation.2 | async-start | bytes 4194304 | tf_op jit(solution)/shard_map/all_to_all | solution.py:16
  395.1 11.8 %copy-start.39 = (bf16[32,16,128]{2,1,0:T(8,128)(2,1)S(1)}, bf16[32,16,128]{2,1,0:T(8,128)(2,1)}, u32[]{:S(2)}) copy-start(bf16[32,16,128]{2,1,0:T(8,128)(2,1)} %get-tuple-element.17) | copy-start | bytes 393220
  395.1 13.2 %copy-start.14 = (bf16[4,128,16,128]{3,1,2,0:T(8,128)(2,1)S(1)}, bf16[4,128,16,128]{3,1,2,0:T(8,128)(2,1)}, u32[]{:S(2)}) copy-start(bf16[4,128,16,128]{3,1,2,0:T(8,128)(2,1)} %all_to_all.90) | copy-start | bytes 6291460
  395.1 56.3 %all-to-all-start.5 = ((bf16[16,32,16,128]{3,1,2,0:T(8,128)(2,1)}), bf16[16,32,16,128]{3,1,2,0:T(8,128)(2,1)}, u32[]{:S(2)}, u32[]{:S(2)}) async-start(bf16[16,32,16,128]{3,1,2,0:T(8,128)(2,1)} %stack.41), calls=%async_computation.5 | async-start | bytes 4194304 | tf_op jit(solution)/shard_map/all_to_all | solution.py:16
  403.8 4.7 copy-start.57
  403.9 4.5 copy-start.58
  410.2 2.7 copy-start.45
  412.3 3.3 copy-start.42
  416.9 4.5 copy-start.44
  423.2 4.9 copy-start.9
  454.1 94.0 %all-to-all-start.14 = ((bf16[16,32,16,128]{3,1,2,0:T(8,128)(2,1)}), bf16[16,32,16,128]{3,1,2,0:T(8,128)(2,1)}, u32[]{:S(2)}, u32[]{:S(2)}) async-start(bf16[16,32,16,128]{3,1,2,0:T(8,128)(2,1)} %stack.50), calls=%async_computation.14 | async-start | bytes 4194304 | tf_op jit(solution)/shard_map/all_to_all | solution.py:16
  479.7 6.5 copy-start.51
  479.7 6.5 copy-start.52
  479.7 6.5 copy-start.53
  479.7 6.5 copy-start.54
  509.9 6.0 copy-start.64
  509.9 6.0 copy-start.65
  548.8 10.3 %all-to-all-start.7 = ((f32[4,128,16]{1,2,0:T(8,128)}), f32[4,128,16]{1,2,0:T(8,128)}, u32[]{:S(2)}, u32[]{:S(2)}) async-start(f32[4,128,16]{1,2,0:T(8,128)} %stack.43), calls=%async_computation.7 | async-start | bytes 65536 | tf_op jit(solution)/shard_map/all_to_all | solution.py:16
  559.7 9.6 %all-to-all-start.9 = ((f32[4,128,16]{1,2,0:T(8,128)}), f32[4,128,16]{1,2,0:T(8,128)}, u32[]{:S(2)}, u32[]{:S(2)}) async-start(f32[4,128,16]{1,2,0:T(8,128)} %stack.45), calls=%async_computation.9 | async-start | bytes 65536 | tf_op jit(solution)/shard_map/all_to_all | solution.py:16
  569.3 14.1 %all-to-all-start.11 = ((f32[8,1,1024]{2,1,0:T(1,128)}), f32[8,1,1024]{2,1,0:T(1,128)}, u32[]{:S(2)}, u32[]{:S(2)}) async-start(f32[8,1,1024]{2,1,0:T(1,128)} %reshape.1066), calls=%async_computation.11 | async-start | bytes 65536 | tf_op jit(solution)/shard_map/all_to_all | solution.py:16
  583.4 12.0 %all-to-all-start.13 = ((f32[8,1,1024]{2,1,0:T(1,128)}), f32[8,1,1024]{2,1,0:T(1,128)}, u32[]{:S(2)}, u32[]{:S(2)}) async-start(f32[8,1,1024]{2,1,0:T(1,128)} %reshape.1064), calls=%async_computation.13 | async-start | bytes 65536 | tf_op jit(solution)/shard_map/all_to_all | solution.py:16
  595.3 11.8 %all-to-all-start.15 = ((f32[16,1,512]{2,1,0:T(1,128)}), f32[16,1,512]{2,1,0:T(1,128)}, u32[]{:S(2)}, u32[]{:S(2)}) async-start(f32[16,1,512]{2,1,0:T(1,128)} %reshape.1060), calls=%async_computation.15 | async-start | bytes 65536 | tf_op jit(solution)/shard_map/all_to_all | solution.py:16
  607.1 12.6 %all-to-all-start.17 = ((f32[16,1,512]{2,1,0:T(1,128)}), f32[16,1,512]{2,1,0:T(1,128)}, u32[]{:S(2)}, u32[]{:S(2)}) async-start(f32[16,1,512]{2,1,0:T(1,128)} %reshape.1062), calls=%async_computation.17 | async-start | bytes 65536 | tf_op jit(solution)/shard_map/all_to_all | solution.py:16
  622.6 6.6 copy-start.61
  622.6 46.3 %all-to-all-start.8 = ((bf16[4,128,16,128]{1,3,2,0:T(8,128)(2,1)}), bf16[4,128,16,128]{1,3,2,0:T(8,128)(2,1)}, u32[]{:S(2)}, u32[]{:S(2)}) async-start(bf16[4,128,16,128]{1,3,2,0:T(8,128)(2,1)} %stack.44), calls=%async_computation.8 | async-start | bytes 4194304 | tf_op jit(solution)/shard_map/all_to_all | solution.py:16
  671.8 53.7 %all-to-all-start.12 = ((bf16[8,64,16,128]{3,1,2,0:T(8,128)(2,1)}), bf16[8,64,16,128]{3,1,2,0:T(8,128)(2,1)}, u32[]{:S(2)}, u32[]{:S(2)}) async-start(bf16[8,64,16,128]{3,1,2,0:T(8,128)(2,1)} %stack.48), calls=%async_computation.12 | async-start | bytes 4194304 | tf_op jit(solution)/shard_map/all_to_all | solution.py:16
  676.2 3.3 copy-start.19
  676.2 3.3 copy-start.63
  728.2 83.5 %all-to-all-start.16 = ((bf16[16,32,16,128]{3,1,2,0:T(8,128)(2,1)}), bf16[16,32,16,128]{3,1,2,0:T(8,128)(2,1)}, u32[]{:S(2)}, u32[]{:S(2)}) async-start(bf16[16,32,16,128]{3,1,2,0:T(8,128)(2,1)} %stack.52), calls=%async_computation.16 | async-start | bytes 4194304 | tf_op jit(solution)/shard_map/all_to_all | solution.py:16
  733.9 4.5 copy-start.13
  738.7 2.9 copy-start.3
  750.7 7.3 copy-start.46
  764.4 13.9 %copy-start.5 = (bf16[16,32,16,128]{3,1,0,2:T(8,128)(2,1)}, bf16[16,32,16,128]{3,1,0,2:T(8,128)(2,1)S(1)}, u32[]{:S(2)}) copy-start(bf16[16,32,16,128]{3,1,0,2:T(8,128)(2,1)S(1)} %copy.419) | copy-start | bytes 6291460
  798.7 3.3 copy-start.2
  (36 other events, 58.2 us)
